TPU v7x, 32 devices: a whole 2x2x4 slice. The times are simulated.
32 devices in a mesh: led: 4 (over y, x), row: 8 (over z, core).
Axes of the slice: x: 2, y: 2, z: 4, core: 2. Of those that a mesh axis runs over, the one named last changes fastest.
Arguments:
- spectrum: float32 [2, 4096, 4096], P(None, 'led', 'row'), may hold values from -6 to 6
- amplitudes: float32 [4, 2048, 2048], P('led', 'row'), may hold values from 0.2 to 3
- offsets: int32 [4, 2], replicated, may hold values from 0 to 2048
- coeffs: float32 [6], replicated, may hold values from -2.5 to 2.5
Outputs:
- updated: float32 [2, 4096, 4096], P(None, 'led', 'row')
All inputs are finite; a program needn't handle non-finite values.
Results may differ from a plain program's by a relative error of at most 0.0001.
Values sent between devices are 32-bit elements; how exact they have to be, the bound alone decides.
No kernel may reach another device: no remote copies, remote signals or barrier semaphores. Data moves between devices by JAX's collectives and lax.ppermute only.
A program may use at most 128 MiB of HBM per device.

v0:
```python
import math
import jax
import jax.numpy as jnp
from jax import lax
from jax.sharding import PartitionSpec as P

SOFTENING = 0.1
HIGHEST_PRECISION = lax.Precision.HIGHEST


def pupil_at(down_index, across_index, coeffs, centre):
    offset_down = down_index - centre
    offset_across = across_index - centre
    inside = offset_down * offset_down + offset_across * offset_across < centre * centre
    upper_norm = offset_down.astype(jnp.float32) * (1.0 / centre)
    lateral = offset_across.astype(jnp.float32) * (1.0 / centre)
    radial = upper_norm * upper_norm + lateral * lateral
    phases = (
        coeffs[0] * (2.0 * radial - 1.0)
        + coeffs[1] * (upper_norm * upper_norm - lateral * lateral)
        + coeffs[2] * (2.0 * upper_norm * lateral)
        + (3.0 * radial - 2.0) * (coeffs[3] * upper_norm + coeffs[4] * lateral)
        + coeffs[5] * (6.0 * radial * radial - 6.0 * radial + 1.0)
    )
    weight = jnp.where(inside, 1.0, 0.0).astype(jnp.float32)
    return (weight * jnp.cos(phases), weight * jnp.sin(phases))


def tables(outer_size, inner_size, direction):
    length = outer_size * inner_size
    angle_step = direction * 2.0 * math.pi / length
    first_index = jnp.arange(outer_size, dtype=jnp.int32)
    grid_first = first_index[:, None] * first_index[None, :] * inner_size % length
    angles_first = grid_first.astype(jnp.float32) * angle_step
    index_k = jnp.arange(outer_size, dtype=jnp.int32)[:, None, None]
    index_r = jnp.arange(inner_size, dtype=jnp.int32)[None, :, None]
    index_j = jnp.arange(inner_size, dtype=jnp.int32)[None, None, :]
    grid_second = index_r * (index_k + outer_size * index_j) % length
    angles_second = grid_second.astype(jnp.float32) * angle_step
    return (
        jnp.cos(angles_first),
        jnp.sin(angles_first),
        jnp.cos(angles_second),
        jnp.sin(angles_second),
    )


def transform(paired, inputs, middle, output, outer_size, inner_size, direction):
    first_re, first_im, second_re, second_im = tables(outer_size, inner_size, direction)
    scaling = 1.0 / math.sqrt(outer_size * inner_size)
    first_table = jnp.stack([jnp.stack([first_re, first_im]), jnp.stack([-first_im, first_re])])
    second_table = (
        jnp.stack([jnp.stack([second_re, second_im]), jnp.stack([-second_im, second_re])]) * scaling
    )
    middle_pair = jnp.einsum(
        "p" + inputs + ",pqtk->q" + middle, paired, first_table, precision=HIGHEST_PRECISION
    )
    return jnp.einsum(
        "p" + middle + ",pqkrj->q" + output, middle_pair, second_table, precision=HIGHEST_PRECISION
    )


def correct(field_re, field_im, measured):
    magnitude = jnp.sqrt(field_re * field_re + field_im * field_im + SOFTENING)
    factor = measured / magnitude
    return (field_re * factor - field_re, field_im * factor - field_im)


def on_device(spectrum, amplitudes, offsets, coeffs):
    led_count = lax.axis_size("led")
    row_count = lax.axis_size("row")
    led_index = lax.axis_index("led")
    row_index = lax.axis_index("row")
    size_rows = spectrum.shape[1]
    size_cols = spectrum.shape[2]
    window = amplitudes.shape[2]
    centre = window // 2
    block_rows = window // row_count
    outer_rows = window // led_count
    outer_cols = window // row_count
    row_shift = offsets[led_index, 0]
    col_shift = offsets[led_index, 1]
    measured = amplitudes[0]
    shape_cols = (2, block_rows, outer_cols, row_count)
    region = lax.all_gather(spectrum, "led", axis=1, tiled=True)
    band_rows = lax.dynamic_slice_in_dim(region, row_shift, window, 1)
    row_ids = jnp.arange(window, dtype=jnp.int32)[:, None]
    col_ids = (row_index * size_cols + jnp.arange(size_cols, dtype=jnp.int32))[None, :] - col_shift
    pupil_re, pupil_im = pupil_at(row_ids, col_ids, coeffs, centre)
    lit_re = pupil_re * band_rows[0] - pupil_im * band_rows[1]
    lit_im = pupil_re * band_rows[1] + pupil_im * band_rows[0]
    shape_rows = (2, outer_rows, led_count, size_cols)
    half = transform(
        jnp.stack([lit_re, lit_im]).reshape(shape_rows),
        "trc",
        "krc",
        "jkc",
        outer_rows,
        led_count,
        1.0,
    )
    stacked = half.reshape(2, window, size_cols)
    spread = lax.all_to_all(stacked, "row", split_axis=1, concat_axis=2, tiled=True)
    window_part = lax.dynamic_slice_in_dim(spread, col_shift, window, 2)
    field = transform(
        window_part.reshape(shape_cols), "ytr", "ykr", "yjk", outer_cols, row_count, 1.0
    )
    field = field.reshape(2, block_rows, window)
    diff_re, diff_im = correct(field[0], field[1], measured)
    back = transform(
        jnp.stack([diff_re, diff_im]).reshape(shape_cols),
        "ytr",
        "ykr",
        "yjk",
        outer_cols,
        row_count,
        -1.0,
    )
    padded = jnp.zeros((2, block_rows, row_count * size_cols), jnp.float32)
    padded = lax.dynamic_update_slice_in_dim(
        padded, back.reshape(2, block_rows, window), col_shift, 2
    )
    gathered_cols = lax.all_to_all(padded, "row", split_axis=2, concat_axis=1, tiled=True)
    spec = transform(
        gathered_cols.reshape(shape_rows), "trc", "krc", "jkc", outer_rows, led_count, -1.0
    ).reshape(2, window, size_cols)
    upd_re = pupil_re * spec[0] + pupil_im * spec[1]
    upd_im = pupil_re * spec[1] - pupil_im * spec[0]
    embedded = jnp.zeros((2, size_rows * led_count, size_cols), jnp.float32)
    embedded = lax.dynamic_update_slice_in_dim(embedded, jnp.stack([upd_re, upd_im]), row_shift, 1)
    summed = lax.psum_scatter(embedded, "led", scatter_dimension=1, tiled=True)
    return spectrum + summed


def solution(mesh):
    return jax.shard_map(
        on_device,
        mesh=mesh,
        in_specs=(P(None, "led", "row"), P("led", "row", None), P(), P()),
        out_specs=P(None, "led", "row"),
        check_vma=False,
    )
```

profile of v0, /device:TPU:0, one launch (start us, length us, event | category | flops | bytes accessed | tf_op | source)
XLA Modules:
  0.0 1087.1 jit_solution(2746678404710610124)
XLA Ops:
  27.8 141.4 %all-gather.2.cloned.1.call-done = f32[2,4096,512]{2,1,0:T(8,128)} async-done(((f32[2,1024,512]{2,1,0:T(8,128)}), f32[2,4096,512]{2,1,0:T(8,128)}) %all-gather.2.cloned.1.call-update) | async-done | bytes 16777232 | tf_op jit(solution)/shard_map/all_gather | solution.py:85
  169.3 26.9 %multiply_subtract_fusion = (f32[1,2048,512]{2,1,0:T(8,128)}, f32[1,2048,512]{2,1,0:T(8,128)}) fusion(f32[2,4096,512]{2,1,0:T(8,128)} %all-gather.2.cloned.1.call-done, s32[]{:T(128)S(6)} %select_n.238, s32[]{:T(128)S(6)} %add.718, f32[]{:T(128)} %bitcast.6, f32[512]{0:T(512)S(1)} %get-tuple-element.53, f32[2048]{0:T(1024)S(1)} %get-tuple-element.58, ...), kind=kLoop, calls=%fused_computation.55 | loop fusion | flops 33554432 | bytes 16818200 | tf_op jit(solution)/shard_map/sub | solution.py:90
  196.1 7.9 stack.215
  204.1 5.5 copy.143
  209.6 7.7 stack.216
  221.4 28.3 %fusion.46 = f32[2,512,4,512,1]{3,1,2,0,4:T(8,128)} fusion(f32[1,512,4,512]{3,1,0,2:T(8,128)S(1)} %copy.144, f32[1,512,4,512]{3,1,0,2:T(8,128)S(1)} %copy-done.3, f32[1,2,512,512]{2,3,0,1:T(8,128)S(1)} %copy-done.4, f32[1,2,512,512]{2,3,0,1:T(8,128)S(1)} %get-tuple-element.17), kind=kOutput, calls=%fused_computation.58 | convolution fusion | flops 25772949504 | bytes 20971520 | tf_op jit(solution)/shard_map/ptrc,pqtk->qkrc/dot_general | solution.py:55
  249.7 32.7 %fusion.11 = f32[2,4,512,512]{3,1,0,2:T(4,128)S(1)} fusion(f32[2,2,512,4,4]{3,4,0,1,2:T(4,128)} %copy.145, f32[2,512,4,512,1]{3,1,2,0,4:T(8,128)} %fusion.46), kind=kOutput, calls=%fused_computation.19 | convolution fusion | flops 201326592 | bytes 16908288 | tf_op jit(solution)/shard_map/pkrc,pqkrj->qjkc/dot_general | solution.py:58
  282.4 4.9 copy.147
  287.2 16.5 %copy.148 = f32[2,2048,512]{2,0,1:T(2,128)} copy(f32[2,2048,512]{2,1,0:T(8,128)S(1)} %bitcast.186) | data formatting | bytes 16777216 | tf_op jit(solution)/shard_map/reshape | solution.py:102
  303.7 5.1 all-to-all-start
  327.6 165.1 %all-to-all-done = f32[2,2048,512]{2,0,1:T(2,128)} async-done(((f32[2,2048,512]{2,0,1:T(2,128)}), f32[2,2048,512]{2,0,1:T(2,128)}, u32[]{:S(2)}, u32[]{:S(2)}) %all-to-all-start) | async-done | bytes 8388640 | tf_op jit(solution)/shard_map/all_to_all | solution.py:103
  492.7 8.2 copy.149
  501.0 8.8 copy.150
  509.7 4.5 dynamic-slice_bitcast_fusion
  514.3 5.3 copy.151
  519.5 9.7 fusion.54
  529.3 7.0 fusion.47
  545.6 9.1 fusion.53
  554.8 7.0 fusion.50
  564.2 5.4 broadcast_in_dim.15
  569.6 12.4 %copy_dynamic-update-slice_fusion = f32[2,256,4096]{1,0,2:T(2,128)} fusion(f32[2,256,4096]{1,0,2:T(2,128)} %broadcast_in_dim.15, s32[]{:T(128)S(6)} %select_n.239, f32[2,256,2048]{1,2,0:T(8,128)S(1)} %bitcast.190), kind=kLoop, calls=%fused_computation.52 | loop fusion | bytes 8388612 | tf_op jit(solution)/shard_map/dynamic_update_slice | solution.py:120
  582.1 5.0 all-to-all-start.1
  600.4 170.5 %all-to-all-done.1 = f32[2,256,4096]{1,0,2:T(2,128)} async-done(((f32[2,256,4096]{1,0,2:T(2,128)}), f32[2,256,4096]{1,0,2:T(2,128)}, u32[]{:S(2)}, u32[]{:S(2)}) %all-to-all-start.1) | async-done | bytes 8388640 | tf_op jit(solution)/shard_map/all_to_all | solution.py:123
  770.9 7.3 copy.164
  778.2 13.3 %copy.165 = f32[2,8,256,512]{3,0,2,1:T(2,128)} copy(f32[2,8,256,512]{2,3,1,0:T(8,128)} %bitcast.188) | data formatting | bytes 16777216 | tf_op jit(solution)/shard_map/all_to_all | solution.py:123
  791.5 31.6 %fusion.41 = f32[2,512,4,512,1]{3,1,2,0,4:T(8,128)} fusion(f32[2,512,4,512]{3,0,2,1:T(2,128)} %bitcast.191, f32[1,2,512,512]{2,3,1,0:T(8,128)} %get-tuple-element.16, f32[1,2,512,512]{2,3,1,0:T(8,128)S(1)} %get-tuple-element.15), kind=kOutput, calls=%fused_computation.57 | convolution fusion | flops 25770852352 | bytes 20971520 | tf_op jit(solution)/shard_map/ptrc,pqtk->qkrc/dot_general | solution.py:55
  823.2 32.4 %fusion.14 = f32[2,4,512,512]{3,1,0,2:T(4,128)S(1)} fusion(f32[2,2,512,4,4]{3,4,0,1,2:T(4,128)} %copy.168, f32[2,512,4,512,1]{3,1,2,0,4:T(8,128)} %fusion.41), kind=kOutput, calls=%fused_computation.20 | convolution fusion | flops 201326592 | bytes 16908288 | tf_op jit(solution)/shard_map/pkrc,pqkrj->qjkc/dot_general | solution.py:58
  863.9 23.1 %fusion.32 = (f32[1,2048,512]{2,1,0:T(8,128)S(1)}, f32[1,2048,512]{2,1,0:T(8,128)S(1)}) fusion(f32[1,4,512,512]{3,2,1,0:T(8,128)S(1)} %copy.171, f32[1,4,512,512]{3,2,1,0:T(8,128)S(1)} %copy.170, f32[]{:T(128)} %bitcast.6, f32[512]{0:T(512)S(1)} %get-tuple-element.53, f32[2048]{0:T(1024)S(1)} %get-tuple-element.58, f32[512]{0:T(512)S(1)} %get-tuple-element.54, ...), kind=kLoop, calls=%fused_computation.41 | loop fusion | flops 33554432 | bytes 16818192 | tf_op jit(solution)/shard_map/add | solution.py:127
  891.3 7.9 broadcast_in_dim.12
  899.2 22.7 %dynamic_update_slice.7 = f32[2,4096,512]{2,1,0:T(8,128)} dynamic-update-slice(f32[2,4096,512]{2,1,0:T(8,128)} %broadcast_in_dim.12, f32[2,2048,512]{2,1,0:T(8,128)} %pad_maximum_fusion, s32[]{:T(128)} %constant.100.clone.1, s32[]{:T(128)S(6)} %select_n.238, s32[]{:T(128)} %constant.100.clone.1) | dynamic-update-slice | bytes 16777220 | tf_op jit(solution)/shard_map/dynamic_update_slice | solution.py:130
  921.8 151.7 %reduce-scatter.2.cloned.1.call-done = f32[2,1024,512]{2,1,0:T(8,128)} async-done(((f32[2,4096,512]{2,1,0:T(8,128)}), f32[2,1024,512]{2,1,0:T(8,128)}) %reduce-scatter.2.cloned.1.call-update) | async-done | bytes 4194320 | tf_op jit(solution)/shard_map/reduce_scatter | solution.py:131
  1073.5 6.5 add.717
  (67 shorter events, 76.3 us)
Async XLA Ops:
  6.5 0.7 copy-start.6
  6.5 2.8 copy-start.5
  6.5 162.7 %all-gather.2.cloned.1.call-start = ((), (), s32[]{:S(2)}) async-start(), calls=%async_computation.3 | async-start | bytes 20971520 | tf_op jit(solution)/shard_map/all_gather | solution.py:85
  217.3 3.7 copy-start.3
  217.3 4.1 copy-start.4
  303.7 189.0 %all-to-all-start = ((f32[2,2048,512]{2,0,1:T(2,128)}), f32[2,2048,512]{2,0,1:T(2,128)}, u32[]{:S(2)}, u32[]{:S(2)}) async-start(f32[2,2048,512]{2,0,1:T(2,128)} %copy.148), calls=%async_computation | async-start | bytes 16777216 | tf_op jit(solution)/shard_map/all_to_all | solution.py:103
  519.5 9.7 copy-start.1
  540.8 3.1 copy-start.2
  545.6 9.1 copy-start
  582.1 188.8 %all-to-all-start.1 = ((f32[2,256,4096]{1,0,2:T(2,128)}), f32[2,256,4096]{1,0,2:T(2,128)}, u32[]{:S(2)}, u32[]{:S(2)}) async-start(f32[2,256,4096]{1,0,2:T(2,128)} %copy_dynamic-update-slice_fusion), calls=%async_computation.1 | async-start | bytes 16777216 | tf_op jit(solution)/shard_map/all_to_all | solution.py:123
  587.0 486.5 %reduce-scatter.2.cloned.1.call-start = ((), (), s32[]{:S(2)}) async-start(), calls=%async_computation.4 | async-start | bytes 20971520 | tf_op jit(solution)/shard_map/reduce_scatter | solution.py:131
Sparse Core Ops, SparseCore 0:
  9.2 160.0 all-gather.1
  922.0 151.5 reduce-scatter.1
where the time goes:
time: 1100 us; the launch traced here: 1090 us
  waiting for transfers between devices  630 us (57%)
  local copies, waits for them, and re-layouts  178 us (16%)
  matrix products  158 us (14%)
  other arithmetic  91.9 us (8%)
  between operations  19.3 us (2%)
    all_to_all x1, waiting for transfers between devices, on_device(): lax.all_to_all(padded, 'row', split_axis=2, concat_axis=1, tiled=True)  171 us
    all_to_all x1, waiting for transfers between devices, on_device(): lax.all_to_all(stacked, 'row', split_axis=1, concat_axis=2, tiled=True)  165 us
    reduce_scatter x1, waiting for transfers between devices, on_device(): summed = lax.psum_scatter(embedded, 'led', scatter_dimension=1, tiled=True)  152 us
    all_gather x1, waiting for transfers between devices, on_device(): region = lax.all_gather(spectrum, 'led', axis=1, tiled=True)  141 us
    dot_general x4, matrix products, transform(): jnp.einsum('p' + middle + ',pqkrj->q' + output, middle_pair, second_table...  79.1 us
    dot_general x4, matrix products, transform(): jnp.einsum('p' + inputs + ',pqtk->q' + middle, paired, first_table, preci...  78.8 us
    sub x1, other arithmetic, on_device(): lit_re = pupil_re * band_rows[0] - pupil_im * band_rows[1]  26.9 us
    another operation x4, local copies, waits for them, and re-layouts, on_device(): jnp.stack([lit_re, lit_im]).reshape(shape_rows)  24.9 us
  transfers between devices with their start and end apart: 4, of which 4 were waited for; matrix products, arithmetic and copies ran while one was open for 4% of the time, Pallas kernels for 0%

commit v1 on v0

--- a/solution.py
+++ b/solution.py
@@ -120,7 +120,10 @@
     padded = lax.dynamic_update_slice_in_dim(
         padded, back.reshape(2, block_rows, window), col_shift, 2
     )
-    gathered_cols = lax.all_to_all(padded, "row", split_axis=2, concat_axis=1, tiled=True)
+    gathered_cols = jnp.concatenate(
+        lax.all_to_all(jnp.stack(jnp.split(padded, lax.axis_size("row"), axis=2)), "row", 0, 0),
+        axis=1,
+    )
     spec = transform(
         gathered_cols.reshape(shape_rows), "trc", "krc", "jkc", outer_rows, led_count, -1.0
     ).reshape(2, window, size_cols)

time: 1100 us -> 1190 us (1.082)
  local copies, waits for them, and re-layouts: 178 us -> 270 us
    dynamic_update_slice x1, local copies, waits for them, and re-layouts: 12.4 us -> 92.2 us  [on_device(): lax.dynamic_update_slice_in_dim(padded, back.reshape(2, block_rows, windo...]
    all_to_all x2 -> x0, local copies, waits for them, and re-layouts: 20.6 us -> none  [on_device(): lax.all_to_all(padded, 'row', split_axis=2, concat_axis=1, tiled=True)]
    unnamed x15 -> x22, local copies, waits for them, and re-layouts: 2.37 us -> 20.4 us
where the time goes in v1:
time: 1190 us; the launch traced here: 1180 us
  waiting for transfers between devices  630 us (53%)
  local copies, waits for them, and re-layouts  270 us (23%)
  matrix products  157 us (13%)
  other arithmetic  91.9 us (8%)
  between operations  19.3 us (2%)
    all_to_all x1, waiting for transfers between devices, on_device(): lax.all_to_all(jnp.stack(jnp.split(padded, lax.axis_size('row'), axis=2))...  171 us
    all_to_all x1, waiting for transfers between devices, on_device(): lax.all_to_all(stacked, 'row', split_axis=1, concat_axis=2, tiled=True)  165 us
    reduce_scatter x1, waiting for transfers between devices, on_device(): summed = lax.psum_scatter(embedded, 'led', scatter_dimension=1, tiled=True)  152 us
    all_gather x1, waiting for transfers between devices, on_device(): region = lax.all_gather(spectrum, 'led', axis=1, tiled=True)  141 us
    dynamic_update_slice x1, local copies, waits for them, and re-layouts, on_device(): lax.dynamic_update_slice_in_dim(padded, back.reshape(2, block_rows, windo...  92.2 us
    dot_general x4, matrix products, transform(): jnp.einsum('p' + middle + ',pqkrj->q' + output, middle_pair, second_table...  79.1 us
    dot_general x4, matrix products, transform(): jnp.einsum('p' + inputs + ',pqtk->q' + middle, paired, first_table, preci...  78.4 us
    sub x1, other arithmetic, on_device(): lit_re = pupil_re * band_rows[0] - pupil_im * band_rows[1]  26.9 us
  transfers between devices with their start and end apart: 4, of which 4 were waited for; matrix products, arithmetic and copies ran while one was open for 4% of the time, Pallas kernels for 0%

profile of v1, /device:TPU:0, one launch (start us, length us, event | category | flops | bytes accessed | tf_op | source)
XLA Modules:
  0.0 1178.1 jit_solution(17854127729474891173)
XLA Ops:
  27.8 141.4 %all-gather.2.cloned.1.call-done = f32[2,4096,512]{2,1,0:T(8,128)} async-done(((f32[2,1024,512]{2,1,0:T(8,128)}), f32[2,4096,512]{2,1,0:T(8,128)}) %all-gather.2.cloned.1.call-update) | async-done | bytes 16777232 | tf_op jit(solution)/shard_map/all_gather | solution.py:85
  169.3 26.9 %multiply_subtract_fusion = (f32[1,2048,512]{2,1,0:T(8,128)}, f32[1,2048,512]{2,1,0:T(8,128)}) fusion(f32[2,4096,512]{2,1,0:T(8,128)} %all-gather.2.cloned.1.call-done, s32[]{:T(128)S(6)} %select_n.238, s32[]{:T(128)S(6)} %add.718, f32[]{:T(128)} %bitcast.6, f32[512]{0:T(512)S(1)} %get-tuple-element.55, f32[2048]{0:T(1024)S(1)} %get-tuple-element.58, ...), kind=kLoop, calls=%fused_computation.54 | loop fusion | flops 33554432 | bytes 16818200 | tf_op jit(solution)/shard_map/sub | solution.py:90
  196.1 7.9 stack.242
  204.1 5.5 copy.86
  209.6 7.7 stack.243
  221.4 28.3 %fusion.46 = f32[2,512,4,512,1]{3,1,2,0,4:T(8,128)} fusion(f32[1,512,4,512]{3,1,0,2:T(8,128)S(1)} %copy.87, f32[1,512,4,512]{3,1,0,2:T(8,128)S(1)} %copy-done.3, f32[1,2,512,512]{2,3,0,1:T(8,128)S(1)} %copy-done.4, f32[1,2,512,512]{2,3,0,1:T(8,128)S(1)} %get-tuple-element.17), kind=kOutput, calls=%fused_computation.57 | convolution fusion | flops 25772949504 | bytes 20971520 | tf_op jit(solution)/shard_map/ptrc,pqtk->qkrc/dot_general | solution.py:55
  249.7 32.7 %fusion.11 = f32[2,4,512,512]{3,1,0,2:T(4,128)S(1)} fusion(f32[2,2,512,4,4]{3,4,0,1,2:T(4,128)} %copy.88, f32[2,512,4,512,1]{3,1,2,0,4:T(8,128)} %fusion.46), kind=kOutput, calls=%fused_computation.19 | convolution fusion | flops 201326592 | bytes 16908288 | tf_op jit(solution)/shard_map/pkrc,pqkrj->qjkc/dot_general | solution.py:58
  282.4 4.9 copy.90
  287.3 16.5 %copy.91 = f32[2,2048,512]{2,0,1:T(2,128)} copy(f32[2,2048,512]{2,1,0:T(8,128)S(1)} %bitcast.217) | data formatting | bytes 16777216 | tf_op jit(solution)/shard_map/reshape | solution.py:102
  303.7 5.1 all-to-all-start
  327.6 165.1 %all-to-all-done = f32[2,2048,512]{2,0,1:T(2,128)} async-done(((f32[2,2048,512]{2,0,1:T(2,128)}), f32[2,2048,512]{2,0,1:T(2,128)}, u32[]{:S(2)}, u32[]{:S(2)}) %all-to-all-start) | async-done | bytes 8388640 | tf_op jit(solution)/shard_map/all_to_all | solution.py:103
  492.7 8.2 copy.92
  501.0 8.8 copy.93
  509.8 4.5 dynamic-slice_bitcast_fusion
  514.3 5.3 copy.94
  519.5 9.7 fusion.54
  529.3 7.0 fusion.47
  545.6 9.1 fusion.53
  554.8 7.0 fusion.50
  561.8 4.4 copy.105
  566.2 7.4 copy.106
  573.6 7.5 broadcast_in_dim.15
  581.2 92.2 %dynamic_update_slice.6 = f32[2,256,4096]{2,0,1:T(2,128)} dynamic-update-slice(f32[2,256,4096]{2,0,1:T(2,128)} %broadcast_in_dim.15, f32[2,256,2048]{2,0,1:T(2,128)} %copy.106, s32[]{:T(128)} %constant.100.clone.1, s32[]{:T(128)} %constant.100.clone.1, s32[]{:T(128)S(6)} %select_n.239) | dynamic-update-slice | bytes 8388612 | tf_op jit(solution)/shard_map/dynamic_update_slice | solution.py:120
  694.0 5.0 all-to-all-start.1
  712.3 170.5 %all-to-all-done.1 = f32[8,2,256,512]{3,1,2,0:T(2,128)} async-done(((f32[8,2,256,512]{3,1,2,0:T(2,128)}), f32[8,2,256,512]{3,1,2,0:T(2,128)}, u32[]{:S(2)}, u32[]{:S(2)}) %all-to-all-start.1) | async-done | bytes 8388640 | tf_op jit(solution)/shard_map/all_to_all | solution.py:124
  882.8 31.2 %fusion.41 = f32[2,512,4,512,1]{3,1,2,0,4:T(8,128)} fusion(f32[2,512,4,512]{3,0,2,1:T(2,128)} %bitcast.75, f32[1,2,512,512]{2,3,1,0:T(8,128)} %get-tuple-element.16, f32[1,2,512,512]{2,3,1,0:T(8,128)S(1)} %get-tuple-element.15), kind=kOutput, calls=%fused_computation.56 | convolution fusion | flops 25770852352 | bytes 20971520 | tf_op jit(solution)/shard_map/ptrc,pqtk->qkrc/dot_general | solution.py:55
  914.1 32.4 %fusion.14 = f32[2,4,512,512]{3,1,0,2:T(4,128)S(1)} fusion(f32[2,2,512,4,4]{3,4,0,1,2:T(4,128)} %copy.109, f32[2,512,4,512,1]{3,1,2,0,4:T(8,128)} %fusion.41), kind=kOutput, calls=%fused_computation.20 | convolution fusion | flops 201326592 | bytes 16908288 | tf_op jit(solution)/shard_map/pkrc,pqkrj->qjkc/dot_general | solution.py:58
  954.8 23.1 %fusion.32 = (f32[1,2048,512]{2,1,0:T(8,128)S(1)}, f32[1,2048,512]{2,1,0:T(8,128)S(1)}) fusion(f32[1,4,512,512]{3,2,1,0:T(8,128)S(1)} %copy.112, f32[1,4,512,512]{3,2,1,0:T(8,128)S(1)} %copy.111, f32[]{:T(128)} %bitcast.6, f32[512]{0:T(512)S(1)} %get-tuple-element.55, f32[2048]{0:T(1024)S(1)} %get-tuple-element.58, f32[512]{0:T(512)S(1)} %get-tuple-element.56, ...), kind=kLoop, calls=%fused_computation.41 | loop fusion | flops 33554432 | bytes 16818192 | tf_op jit(solution)/shard_map/add | solution.py:130
  982.2 7.9 broadcast_in_dim.12
  990.1 22.7 %dynamic_update_slice.7 = f32[2,4096,512]{2,1,0:T(8,128)} dynamic-update-slice(f32[2,4096,512]{2,1,0:T(8,128)} %broadcast_in_dim.12, f32[2,2048,512]{2,1,0:T(8,128)} %pad_maximum_fusion, s32[]{:T(128)} %constant.100.clone.1, s32[]{:T(128)S(6)} %select_n.238, s32[]{:T(128)} %constant.100.clone.1) | dynamic-update-slice | bytes 16777220 | tf_op jit(solution)/shard_map/dynamic_update_slice | solution.py:133
  1012.7 151.8 %reduce-scatter.2.cloned.1.call-done = f32[2,1024,512]{2,1,0:T(8,128)} async-done(((f32[2,4096,512]{2,1,0:T(8,128)}), f32[2,1024,512]{2,1,0:T(8,128)}) %reduce-scatter.2.cloned.1.call-update) | async-done | bytes 4194320 | tf_op jit(solution)/shard_map/reduce_scatter | solution.py:134
  1164.5 6.5 add.717
  (74 shorter events, 94.5 us)
Async XLA Ops:
  6.5 0.7 copy-start.6
  6.5 2.8 copy-start.5
  6.5 162.7 %all-gather.2.cloned.1.call-start = ((), (), s32[]{:S(2)}) async-start(), calls=%async_computation.3 | async-start | bytes 20971520 | tf_op jit(solution)/shard_map/all_gather | solution.py:85
  217.3 3.7 copy-start.3
  217.3 4.1 copy-start.4
  303.7 189.0 %all-to-all-start = ((f32[2,2048,512]{2,0,1:T(2,128)}), f32[2,2048,512]{2,0,1:T(2,128)}, u32[]{:S(2)}, u32[]{:S(2)}) async-start(f32[2,2048,512]{2,0,1:T(2,128)} %copy.91), calls=%async_computation | async-start | bytes 16777216 | tf_op jit(solution)/shard_map/all_to_all | solution.py:103
  519.5 9.7 copy-start.1
  540.8 3.1 copy-start.2
  545.6 9.1 copy-start
  694.0 188.8 %all-to-all-start.1 = ((f32[8,2,256,512]{3,1,2,0:T(2,128)}), f32[8,2,256,512]{3,1,2,0:T(2,128)}, u32[]{:S(2)}, u32[]{:S(2)}) async-start(f32[8,2,256,512]{3,1,2,0:T(2,128)} %fusion.65), calls=%async_computation.1 | async-start | bytes 16777216 | tf_op jit(solution)/shard_map/all_to_all | solution.py:124
  699.0 465.5 %reduce-scatter.2.cloned.1.call-start = ((), (), s32[]{:S(2)}) async-start(), calls=%async_computation.4 | async-start | bytes 20971520 | tf_op jit(solution)/shard_map/reduce_scatter | solution.py:134
Sparse Core Ops, SparseCore 0:
  9.2 160.0 all-gather.1
  1012.9 151.6 reduce-scatter.1
